TPU v7x, 512 devices: a whole 4x8x8 slice. The times are simulated.
512 devices in a mesh: dp: 16 (over z, core), mp: 32 (over x, y).
Axes of the slice: x: 4, y: 8, z: 8, core: 2. Of those that a mesh axis runs over, the one named last changes fastest.
Arguments:
- tokens: bfloat16 [2048, 4096], P(('dp', 'mp')), may hold values from -6 to 6
- hidden_grad: bfloat16 [2048, 14336], P('dp', 'mp'), may hold values from -0.125 to 0.125
- gate_weight: bfloat16 [4096, 14336], P('dp', 'mp'), may hold values from -0.09375 to 0.09375
- up_weight: bfloat16 [4096, 14336], P('dp', 'mp'), may hold values from -0.09375 to 0.09375
- gate_probe: bfloat16 [4096, 14336], P('dp', 'mp'), may hold values from -1 to 1, as said below
- gate_mean: float32 [4096, 14336], P('dp', 'mp'), may hold values from -0.6 to 0.6
- gate_curve: float32 [4096, 14336], P('dp', 'mp'), may hold values from 1 to 10
- group_counts: int32 [16], replicated, may hold values from 32 to 128, as said below
Outputs:
- gate_weight_new: bfloat16 [4096, 14336], P('dp', 'mp')
- gate_mean_new: float32 [4096, 14336], P('dp', 'mp')
- gate_curve_new: float32 [4096, 14336], P('dp', 'mp')
Inputs may be any that keep to these rules, and one draw needn't show every extreme that they name: `group_counts`: some data group has exactly 128 live tokens in every draw. `gate_probe`: every entry is -1 or 1, each sign drawn independently.
All inputs are finite; a program needn't handle non-finite values.
Results may differ from a plain program's by a relative error of at most 0.0017.
Values may be sent and summed in bfloat16 or wider, within the bound.
No kernel may reach another device: no remote copies, remote signals or barrier semaphores. Data moves between devices by JAX's collectives and lax.ppermute only.
A program may use at most 64 MiB of HBM per device.

v0:
```python
import jax
import jax.numpy as jnp
from jax import lax
from jax.sharding import PartitionSpec as P

first_decay = 0.9
second_decay = 0.999
learn_rate = 0.15
epsilon_term = 0.0001
first_fix = 1.0 - 0.9**10
second_fix = 1.0 - 0.999**10


def silu_parts(inputs):
    sigmoid_part = jax.nn.sigmoid(inputs)
    silu_slope = sigmoid_part * (1.0 + inputs * (1.0 - sigmoid_part))
    silu_bend = sigmoid_part * (1.0 - sigmoid_part) * (2.0 + inputs * (1.0 - 2.0 * sigmoid_part))
    return (silu_slope, silu_bend)


def adahessian(weight, mean_old, curve_old, gradient, probe_value, product):
    diagonal = probe_value.astype(jnp.float32) * product
    mean_new = first_decay * mean_old + (1.0 - first_decay) * gradient
    curve_new = second_decay * curve_old + (1.0 - second_decay) * diagonal * diagonal
    step_ratio = mean_new / first_fix / (jnp.sqrt(curve_new / second_fix) + epsilon_term)
    weight_new = (weight.astype(jnp.float32) - learn_rate * step_ratio).astype(jnp.bfloat16)
    return (weight_new, mean_new, curve_new)


def body(
    tokens, hidden_grad, gate_weight, up_weight, gate_probe, gate_mean, gate_curve, group_counts
):
    whole = lax.all_gather(tokens, "mp", axis=0, tiled=True)
    columns = lax.all_to_all(whole, "dp", split_axis=1, concat_axis=0, tiled=True)
    group_rows = whole.shape[0]
    width = gate_weight.shape[1]
    pieces = (
        lax.all_gather(gate_weight, "dp", axis=0, tiled=True),
        lax.all_gather(up_weight, "dp", axis=0, tiled=True),
    )
    gate_pre, up_pre = tuple(
        (jnp.dot(whole, piece, preferred_element_type=jnp.float32) for piece in pieces)
    )
    selected = columns
    gate_tan = lax.psum_scatter(
        jnp.dot(selected, gate_probe, preferred_element_type=jnp.float32),
        "dp",
        scatter_dimension=0,
        tiled=True,
    )
    group_index = lax.axis_index("dp")
    limit = lax.dynamic_index_in_dim(group_counts, group_index, 0, keepdims=False)
    live = (jnp.arange(group_rows, dtype=jnp.int32) < limit).astype(jnp.float32)
    silu_slope, silu_bend = silu_parts(gate_pre)
    masked = hidden_grad.astype(jnp.float32) * live[:, None]
    grad_gate = (masked * up_pre * silu_slope).astype(jnp.bfloat16)
    tan_gate = (masked * up_pre * silu_bend * gate_tan).astype(jnp.bfloat16)
    packed = jnp.concatenate([grad_gate, tan_gate], 1)
    selected = columns
    sums = lax.dot_general(
        selected,
        lax.all_gather(packed, "dp", axis=0, tiled=True),
        (((0,), (0,)), ((), ())),
        preferred_element_type=jnp.float32,
    )
    gate_out = adahessian(
        gate_weight, gate_mean, gate_curve, sums[:, :width], gate_probe, sums[:, width:]
    )
    return (gate_out[0], gate_out[1], gate_out[2])


def solution(mesh):
    return jax.shard_map(
        body,
        mesh=mesh,
        in_specs=(
            P(("dp", "mp"), None),
            P("dp", "mp"),
            P("dp", "mp"),
            P("dp", "mp"),
            P("dp", "mp"),
            P("dp", "mp"),
            P("dp", "mp"),
            P(),
        ),
        out_specs=(P("dp", "mp"), P("dp", "mp"), P("dp", "mp")),
        check_vma=False,
    )
```

profile of v0, /device:TPU:1, one launch (start us, length us, event | category | flops | bytes accessed | tf_op | source)
XLA Modules:
  0.0 342.0 jit_solution(2087898380235495970)
XLA Ops:
  7.2 0.0 copy-start.2
  7.2 0.0 all-gather.12.cloned.1.call-start
  7.2 0.7 all-gather.12.cloned.1.call-update
  7.9 0.0 all-gather.8.cloned.1.call-start
  8.0 0.7 all-gather.8.cloned.1.call-update
  8.7 0.0 all-gather.6.cloned.1.call-start
  8.7 0.7 all-gather.6.cloned.1.call-update
  9.4 0.0 reduce-scatter.2.cloned.1.call-start
  9.4 83.9 %all-gather.12.cloned.1.call-done = bf16[32,4,4096]{2,1,0:T(4,128)(2,1)} async-done(((bf16[1,4,4096]{2,1,0:T(4,128)(2,1)}), bf16[32,4,4096]{2,1,0:T(4,128)(2,1)}) %all-gather.12.cloned.1.call-update) | async-done | bytes 1048592 | tf_op jit(solution)/shard_map/all_gather | solution.py:33
  93.3 1.8 all_to_all.14
  95.1 0.3 copy.12
  95.5 47.8 %all_to_all.19 = bf16[128,16,256]{2,0,1:T(8,128)(2,1)S(1)} all-to-all(bf16[128,16,256]{2,0,1:T(8,128)(2,1)S(1)} %copy.12), channel_id=1, replica_groups=mesh['dp'=16,'mp'=32] {'dp'}, dimensions={1} | all-to-all | bytes 2097152 | tf_op jit(solution)/shard_map/all_to_all | solution.py:34
  143.3 0.0 copy-done.2
  143.3 2.6 fusion.13
  145.9 0.0 copy-start.6
  145.9 0.0 copy-start
  145.9 0.0 reduce-scatter.2.cloned.1.call-update
  145.9 0.0 copy-start.5
  145.9 0.0 all-gather.10.cloned.1.call-start
  146.0 0.6 copy-done.6
  146.5 0.6 dynamic_slice.4
  147.1 0.6 compare_convert_fusion
  147.8 0.0 copy-done
  147.8 0.3 reshape.15
  148.1 15.2 %all-gather.8.cloned.1.call-done = bf16[4096,448]{0,1:T(8,128)(2,1)} async-done(((bf16[256,448]{0,1:T(8,128)(2,1)}), bf16[4096,448]{0,1:T(8,128)(2,1)}) %all-gather.8.cloned.1.call-update) | async-done | bytes 3670032 | tf_op jit(solution)/shard_map/all_gather | solution.py:38
  163.3 3.1 fusion.12
  166.5 45.4 %all-gather.6.cloned.1.call-done = bf16[4096,448]{0,1:T(8,128)(2,1)} async-done(((bf16[256,448]{0,1:T(8,128)(2,1)}), bf16[4096,448]{0,1:T(8,128)(2,1)}) %all-gather.6.cloned.1.call-update) | async-done | bytes 3670032 | tf_op jit(solution)/shard_map/all_gather | solution.py:39
  211.9 63.9 %reduce-scatter.2.cloned.1.call-done = f32[128,448]{0,1:T(8,128)} async-done(((f32[2048,448]{0,1:T(8,128)}), f32[128,448]{0,1:T(8,128)}) %reduce-scatter.2.cloned.1.call-update) | async-done | bytes 229392 | tf_op jit(solution)/shard_map/reduce_scatter | solution.py:45
  275.8 0.0 copy-done.5
  275.8 3.2 fusion.5
  278.9 0.7 pad_maximum_fusion
  279.6 0.0 all-gather.10.cloned.1.call-update
  279.7 0.0 copy-start.1
  279.7 0.0 copy-start.3
  279.7 0.0 copy-start.4
  279.7 51.3 %all-gather.10.cloned.1.call-done = bf16[2048,896]{0,1:T(8,128)(2,1)} async-done(((bf16[128,896]{0,1:T(8,128)(2,1)}), bf16[2048,896]{0,1:T(8,128)(2,1)}) %all-gather.10.cloned.1.call-update) | async-done | bytes 3670032 | tf_op jit(solution)/shard_map/all_gather | solution.py:62
  331.0 3.1 convolution_bitcast_fusion
  334.2 0.0 copy-done.1
  334.2 0.0 copy-done.3
  334.2 0.0 copy-done.4
  334.2 1.2 subtract_convert_fusion
Async XLA Ops:
  7.2 136.1 %copy-start.2 = (bf16[256,448]{0,1:T(8,128)(2,1)S(1)}, bf16[256,448]{0,1:T(8,128)(2,1)}, u32[]{:S(2)}) copy-start(bf16[256,448]{0,1:T(8,128)(2,1)} %param.12) | copy-start | bytes 688132
  7.2 86.2 %all-gather.12.cloned.1.call-start = ((), (), s32[]{:S(2)}) async-start(), calls=%async_computation.6 | async-start | bytes 1081344 | tf_op jit(solution)/shard_map/all_gather | solution.py:33
  7.9 155.4 %all-gather.8.cloned.1.call-start = ((), (), s32[]{:S(2)}) async-start(), calls=%async_computation.3 | async-start | bytes 3899392 | tf_op jit(solution)/shard_map/all_gather | solution.py:38
  8.7 203.2 %all-gather.6.cloned.1.call-start = ((), (), s32[]{:S(2)}) async-start(), calls=%async_computation.2 | async-start | bytes 3899392 | tf_op jit(solution)/shard_map/all_gather | solution.py:39
  9.4 266.4 %reduce-scatter.2.cloned.1.call-start = ((), (), s32[]{:S(2)}) async-start(), calls=%async_computation.4 | async-start | bytes 3899392 | tf_op jit(solution)/shard_map/reduce_scatter | solution.py:45
  145.9 0.7 copy-start.6
  145.9 1.9 copy-start
  145.9 129.9 %copy-start.5 = (bf16[128,448]{0,1:T(8,128)(2,1)S(1)}, bf16[128,448]{0,1:T(8,128)(2,1)}, u32[]{:S(2)}) copy-start(bf16[128,448]{0,1:T(8,128)(2,1)} %param.9) | copy-start | bytes 344068
  145.9 185.1 %all-gather.10.cloned.1.call-start = ((), (), s32[]{:S(2)}) async-start(), calls=%async_computation.5 | async-start | bytes 3899392 | tf_op jit(solution)/shard_map/all_gather | solution.py:62
  279.7 54.5 %copy-start.1 = (bf16[256,448]{0,1:T(8,128)(2,1)S(1)}, bf16[256,448]{0,1:T(8,128)(2,1)}, u32[]{:S(2)}) copy-start(bf16[256,448]{0,1:T(8,128)(2,1)} %param.10) | copy-start | bytes 688132
  279.7 54.5 %copy-start.3 = (f32[256,448]{0,1:T(8,128)S(1)}, f32[256,448]{0,1:T(8,128)}, u32[]{:S(2)}) copy-start(f32[256,448]{0,1:T(8,128)} %param.13) | copy-start | bytes 1376260
  279.7 54.5 %copy-start.4 = (f32[256,448]{0,1:T(8,128)S(1)}, f32[256,448]{0,1:T(8,128)}, u32[]{:S(2)}) copy-start(f32[256,448]{0,1:T(8,128)} %param.14) | copy-start | bytes 1376260
Sparse Core Ops, SparseCore 0:
  11.2 82.1 all-gather.11
  95.4 67.8 all-gather.7
  165.4 46.4 all-gather.5
  214.6 61.1 reduce-scatter.1
  279.8 51.2 all-gather.9
where the time goes:
time: 342 us
  waiting for transfers between devices  262 us (77%)
  blocking collectives  47.8 us (14%)
  between operations  13.9 us (4%)
  matrix products  12 us (4%)
  local copies, waits for them, and re-layouts  3.58 us (1%)
    all_gather x1, waiting for transfers between devices, body(): whole = lax.all_gather(tokens, 'mp', axis=0, tiled=True)  83.9 us
    reduce_scatter x1, waiting for transfers between devices, body(): lax.psum_scatter(jnp.dot(selected, gate_probe, preferred_element_type=jnp...  63.9 us
    all_gather x1, waiting for transfers between devices, body(): lax.all_gather(packed, 'dp', axis=0, tiled=True)  51.3 us
    all_to_all x1, blocking collectives, body(): lax.all_to_all(whole, 'dp', split_axis=1, concat_axis=0, tiled=True)  47.8 us
    all_gather x1, waiting for transfers between devices, body(): lax.all_gather(up_weight, 'dp', axis=0, tiled=True)  45.4 us
    all_gather x1, waiting for transfers between devices, body(): lax.all_gather(gate_weight, 'dp', axis=0, tiled=True)  15.2 us
  transfers between devices with their start and end apart: 5, of which 5 were waited for; matrix products, arithmetic and copies ran while one was open for 2% of the time, Pallas kernels for 0%

commit v1 on v0

--- a/solution.py
+++ b/solution.py
@@ -30,7 +30,9 @@
 def body(
     tokens, hidden_grad, gate_weight, up_weight, gate_probe, gate_mean, gate_curve, group_counts
 ):
-    whole = lax.all_gather(tokens, "mp", axis=0, tiled=True)
+    whole = jnp.concatenate(
+        lax.all_to_all(jnp.stack([tokens] * lax.axis_size("mp")), "mp", 0, 0), axis=0
+    )
     columns = lax.all_to_all(whole, "dp", split_axis=1, concat_axis=0, tiled=True)
     group_rows = whole.shape[0]
     width = gate_weight.shape[1]

time: 342 us -> 259 us (0.76)
  waiting for transfers between devices: 262 us -> 148 us
  blocking collectives: 47.8 us -> 78.3 us
    all_gather x1 -> x0, waiting for transfers between devices: 83.9 us -> none  [body(): whole = lax.all_gather(tokens, 'mp', axis=0, tiled=True)]
    all_to_all x0 -> x1, blocking collectives: none -> 35.2 us  [body(): lax.all_to_all(jnp.stack([tokens] * lax.axis_size('mp')), 'mp', 0, 0)]
    all_gather x1, waiting for transfers between devices: 15.2 us -> 0.02 us  [body(): lax.all_gather(gate_weight, 'dp', axis=0, tiled=True)]
    all_gather x1, waiting for transfers between devices: 45.4 us -> 31 us  [body(): lax.all_gather(up_weight, 'dp', axis=0, tiled=True)]
    all_to_all x1, blocking collectives: 47.8 us -> 43.2 us  [body(): lax.all_to_all(whole, 'dp', split_axis=1, concat_axis=0, tiled=True)]
  transfers between devices with their start and end apart: 5 -> 4, of which waited for: 5 -> 3; matrix products, arithmetic and copies ran while one was open for 2% -> 3% of each run, Pallas kernels for 0% -> 0%
where the time goes in v1:
time: 259 us
  waiting for transfers between devices  148 us (57%)
  blocking collectives  78.3 us (30%)
  between operations  13.9 us (5%)
  matrix products  12 us (5%)
  local copies, waits for them, and re-layouts  3.77 us (1%)
  other arithmetic  2.59 us (1%)
    reduce_scatter x1, waiting for transfers between devices, body(): lax.psum_scatter(jnp.dot(selected, gate_probe, preferred_element_type=jnp...  64.1 us
    all_gather x1, waiting for transfers between devices, body(): lax.all_gather(packed, 'dp', axis=0, tiled=True)  51.3 us
    all_to_all x1, blocking collectives, body(): lax.all_to_all(whole, 'dp', split_axis=1, concat_axis=0, tiled=True)  43.2 us
    all_to_all x1, blocking collectives, body(): lax.all_to_all(jnp.stack([tokens] * lax.axis_size('mp')), 'mp', 0, 0)  35.2 us
    all_gather x1, waiting for transfers between devices, body(): lax.all_gather(up_weight, 'dp', axis=0, tiled=True)  31 us
    dot_general x2, matrix products, body(): jnp.dot(whole, piece, preferred_element_type=jnp.float32)  6.31 us
  transfers between devices with their start and end apart: 4, of which 3 were waited for; matrix products, arithmetic and copies ran while one was open for 3% of the time, Pallas kernels for 0%

profile of v1, /device:TPU:1, one launch (start us, length us, event | category | flops | bytes accessed | tf_op | source)
XLA Modules:
  0.0 258.6 jit_solution(155342898958933534)
XLA Ops:
  7.2 0.0 all-gather.6.cloned.1.call-start
  7.2 0.7 all-gather.6.cloned.1.call-update
  7.9 0.0 all-gather.4.cloned.1.call-start
  7.9 0.7 all-gather.4.cloned.1.call-update
  8.6 0.0 reduce-scatter.2.cloned.1.call-start
  8.7 1.2 stack.2
  9.9 35.2 %all_to_all.24 = bf16[32,4,4096]{2,1,0:T(4,128)(2,1)S(1)} all-to-all(bf16[32,4,4096]{2,1,0:T(4,128)(2,1)S(1)} %stack.2), channel_id=1, replica_groups=mesh['dp'=16,'mp'=32] {'mp'}, dimensions={0} | all-to-all | bytes 2097152 | tf_op jit(solution)/shard_map/all_to_all | solution.py:34
  45.1 0.0 copy-start.1
  45.1 0.8 all_to_all.18
  45.8 0.3 copy.12
  46.2 43.2 %all_to_all.25 = bf16[128,16,256]{2,0,1:T(8,128)(2,1)S(1)} all-to-all(bf16[128,16,256]{2,0,1:T(8,128)(2,1)S(1)} %copy.12), channel_id=1, replica_groups=mesh['dp'=16,'mp'=32] {'dp'}, dimensions={1} | all-to-all | bytes 2097152 | tf_op jit(solution)/shard_map/all_to_all | solution.py:36
  89.4 0.0 copy-done.1
  89.4 2.6 fusion.13
  91.9 0.0 copy-start.5
  91.9 0.0 reduce-scatter.2.cloned.1.call-update
  92.0 0.0 copy-start.4
  92.0 0.0 all-gather.8.cloned.1.call-start
  92.0 0.6 copy-done.5
  92.6 0.6 dynamic_slice.4
  93.2 0.6 compare_convert_fusion
  93.8 0.3 reshape.20
  94.1 0.0 all-gather.6.cloned.1.call-done
  94.2 3.1 %fusion.12 = f32[128,448]{0,1:T(8,128)S(1)} fusion(bf16[128,4096]{1,0:T(8,128)(2,1)S(1)} %reshape.20, bf16[4096,448]{0,1:T(8,128)(2,1)} %all-gather.6.cloned.1.call-done), kind=kOutput, calls=%fused_computation.21 | convolution fusion | flops 469762048 | bytes 4947968 | tf_op jit(solution)/shard_map/dot_general | solution.py:44
  97.3 31.0 %all-gather.4.cloned.1.call-done = bf16[4096,448]{0,1:T(8,128)(2,1)} async-done(((bf16[256,448]{0,1:T(8,128)(2,1)}), bf16[4096,448]{0,1:T(8,128)(2,1)}) %all-gather.4.cloned.1.call-update) | async-done | bytes 3670032 | tf_op jit(solution)/shard_map/all_gather | solution.py:41
  128.3 64.1 %reduce-scatter.2.cloned.1.call-done = f32[128,448]{0,1:T(8,128)} async-done(((f32[2048,448]{0,1:T(8,128)}), f32[128,448]{0,1:T(8,128)}) %reduce-scatter.2.cloned.1.call-update) | async-done | bytes 229392 | tf_op jit(solution)/shard_map/reduce_scatter | solution.py:47
  192.4 0.0 copy-done.4
  192.4 3.2 %fusion.5 = (bf16[128,448]{0,1:T(8,128)(2,1)S(1)}, bf16[128,448]{0,1:T(8,128)(2,1)S(1)}) fusion(f32[128,448]{0,1:T(8,128)S(1)} %fusion.12, f32[128,448]{0,1:T(8,128)} %reduce-scatter.2.cloned.1.call-done, bf16[128,4096]{1,0:T(8,128)(2,1)S(1)} %reshape.20, bf16[4096,448]{0,1:T(8,128)(2,1)} %all-gather.4.cloned.1.call-done, f32[128]{0:T(128)S(1)} %compare_convert_fusion, ...), kind=kOutput, calls=%fused_computation.13 | convolution fusion | flops 470966272 | bytes 5521920 | tf_op jit(solution)/shard_map/dot_general | solution.py:44
  195.6 0.7 pad_maximum_fusion
  196.3 0.0 all-gather.8.cloned.1.call-update
  196.3 0.0 copy-start
  196.3 0.0 copy-start.2
  196.3 0.0 copy-start.3
  196.3 51.3 %all-gather.8.cloned.1.call-done = bf16[2048,896]{0,1:T(8,128)(2,1)} async-done(((bf16[128,896]{0,1:T(8,128)(2,1)}), bf16[2048,896]{0,1:T(8,128)(2,1)}) %all-gather.8.cloned.1.call-update) | async-done | bytes 3670032 | tf_op jit(solution)/shard_map/all_gather | solution.py:64
  247.7 3.1 %convolution_bitcast_fusion = f32[256,896]{0,1:T(8,128)S(1)} fusion(bf16[2048,896]{0,1:T(8,128)(2,1)} %all-gather.8.cloned.1.call-done, bf16[2048,256]{1,0:T(8,128)(2,1)S(1)} %bitcast.15), kind=kOutput, calls=%fused_computation | convolution fusion | flops 939524096 | bytes 5636096 | tf_op jit(solution)/shard_map/dot_general | solution.py:62
  250.8 0.0 copy-done
  250.8 0.0 copy-done.2
  250.8 0.0 copy-done.3
  250.9 1.2 subtract_convert_fusion
Async XLA Ops:
  7.2 87.0 %all-gather.6.cloned.1.call-start = ((), (), s32[]{:S(2)}) async-start(), calls=%async_computation.4 | async-start | bytes 3899392 | tf_op jit(solution)/shard_map/all_gather | solution.py:40
  7.9 120.4 %all-gather.4.cloned.1.call-start = ((), (), s32[]{:S(2)}) async-start(), calls=%async_computation.3 | async-start | bytes 3899392 | tf_op jit(solution)/shard_map/all_gather | solution.py:41
  8.6 183.8 %reduce-scatter.2.cloned.1.call-start = ((), (), s32[]{:S(2)}) async-start(), calls=%async_computation.5 | async-start | bytes 3899392 | tf_op jit(solution)/shard_map/reduce_scatter | solution.py:47
  45.1 44.3 %copy-start.1 = (bf16[256,448]{0,1:T(8,128)(2,1)S(1)}, bf16[256,448]{0,1:T(8,128)(2,1)}, u32[]{:S(2)}) copy-start(bf16[256,448]{0,1:T(8,128)(2,1)} %param.12) | copy-start | bytes 688132
  91.9 0.7 copy-start.5
  92.0 100.4 %copy-start.4 = (bf16[128,448]{0,1:T(8,128)(2,1)S(1)}, bf16[128,448]{0,1:T(8,128)(2,1)}, u32[]{:S(2)}) copy-start(bf16[128,448]{0,1:T(8,128)(2,1)} %param.9) | copy-start | bytes 344068
  92.0 155.7 %all-gather.8.cloned.1.call-start = ((), (), s32[]{:S(2)}) async-start(), calls=%async_computation.6 | async-start | bytes 3899392 | tf_op jit(solution)/shard_map/all_gather | solution.py:64
  196.3 54.5 %copy-start = (bf16[256,448]{0,1:T(8,128)(2,1)S(1)}, bf16[256,448]{0,1:T(8,128)(2,1)}, u32[]{:S(2)}) copy-start(bf16[256,448]{0,1:T(8,128)(2,1)} %param.10) | copy-start | bytes 688132
  196.3 54.5 %copy-start.2 = (f32[256,448]{0,1:T(8,128)S(1)}, f32[256,448]{0,1:T(8,128)}, u32[]{:S(2)}) copy-start(f32[256,448]{0,1:T(8,128)} %param.13) | copy-start | bytes 1376260
  196.3 54.5 %copy-start.3 = (f32[256,448]{0,1:T(8,128)S(1)}, f32[256,448]{0,1:T(8,128)}, u32[]{:S(2)}) copy-start(f32[256,448]{0,1:T(8,128)} %param.14) | copy-start | bytes 1376260
Sparse Core Ops, SparseCore 0:
  10.0 56.0 all-gather.5
  68.2 60.1 all-gather.3
  131.2 61.1 reduce-scatter.1
  196.4 51.1 all-gather.7
